TPU v7x, 32 devices: a whole 2x2x4 slice. The times are simulated.
32 devices in a mesh: region: 4 (over z), sub: 8 (over y, x, core).
Axes of the slice: x: 2, y: 2, z: 4, core: 2. Of those that a mesh axis runs over, the one named last changes fastest.
Arguments:
- feats: bfloat16 [16384, 1536], P(('region', 'sub')), may hold values from -6 to 6
- conv_weight: bfloat16 [192, 128], replicated, may hold values from -0.4375 to 0.4375
- conv_bias: float32 [128], replicated, may hold values from -3 to 3
- theta: bfloat16 [64, 64], replicated, may hold values from -0.75 to 0.75
- edge_weight: float32 [4096], P(('region', 'sub')), may hold values from 1 to 4
- inner_edge: int32 [16384, 2], P(('region', 'sub')), may hold values from 0 to 127
- crossing_segment: int32 [4096], P(('region', 'sub')), may hold values from 0 to 511
- cut_dest: int32 [4096, 1], P(('region', 'sub')), may hold values from 0 to 31; in each aligned block of 128 rows (0 to 127, 128 to 255, ...) at most 8 rows name the same one
- crossing_hyperedge: int32 [4096], P(('region', 'sub')), may hold values from 0 to 127
- cotangent: bfloat16 [16384, 1280], P(('region', 'sub')), may hold values from -6 to 6
Outputs:
- block_out: bfloat16 [16384, 1280], P(('region', 'sub'))
- grad_feats: bfloat16 [16384, 1536], P(('region', 'sub'))
- grad_conv: float32 [192, 128], replicated
- grad_bias: float32 [128], replicated
- grad_theta: float32 [64, 64], replicated
Inputs may be any that keep to these rules, and one draw needn't show every extreme that they name: `cut_dest`: among the 128 cut memberships of one device no owner is named more than 8 times; in some device one owner is named exactly 8 times.
All inputs are finite; a program needn't handle non-finite values.
Results may differ from a plain program's by a relative error of at most 0.0072.
Values may be sent and summed in bfloat16 or wider, within the bound.
No kernel may reach another device: no remote copies, remote signals or barrier semaphores. Data moves between devices by JAX's collectives and lax.ppermute only.
A program may use at most 64 MiB of HBM per device.

v0:
```python
import jax
import jax.numpy as jnp
from jax import lax
from jax.sharding import PartitionSpec as P

C = 64
T_SIZE = 12
B = 2
KT = 3
MEM = 2
TP = 10
EDGE_DEV = 128


def body(
    feats,
    conv_weight,
    conv_bias,
    theta,
    edge_weight,
    inner_edge,
    crossing_segment,
    cut_dest,
    crossing_hyperedge,
    cotangent,
):
    seg = feats.shape[0]
    n_region = lax.axis_size("region")
    n_sub = lax.axis_size("sub")
    device_list = n_region * n_sub
    slot_capacity = max(2, 2 * crossing_segment.shape[0] // device_list)
    slot_total = device_list * slot_capacity
    width = TP * B * C
    x4 = feats.reshape(seg, T_SIZE, B, C)
    stack = jnp.concatenate([x4[:, k : k + TP] for k in range(KT)], axis=-1)
    u = (
        jnp.einsum("stbk,kf->stbf", stack, conv_weight, preferred_element_type=jnp.float32)
        + conv_bias
    )
    gate = jax.nn.sigmoid(u[..., C:])
    first = u[..., :C]
    hidden = (first * gate).astype(jnp.bfloat16)
    z = (
        jnp.einsum("stbc,cd->stbd", hidden, theta, preferred_element_type=jnp.float32)
        .astype(jnp.bfloat16)
        .reshape(seg, width)
    )
    edge_index = jnp.arange(EDGE_DEV, dtype=jnp.int32)
    incidence = jnp.zeros((EDGE_DEV, seg), jnp.float32)
    for m in range(MEM):
        incidence = incidence + (inner_edge[:, m][None, :] == edge_index[:, None]).astype(
            jnp.float32
        )
    inner_count = jnp.sum(incidence, axis=1)
    incidence = incidence.astype(jnp.bfloat16)
    dest = cut_dest[:, 0]
    dest_hot = (dest[:, None] == jnp.arange(device_list, dtype=jnp.int32)[None, :]).astype(
        jnp.int32
    )
    rank = jnp.sum((jnp.cumsum(dest_hot, axis=0) - 1) * dest_hot, axis=1)
    slot_position = dest * slot_capacity + rank
    slotted_segment = jnp.full((slot_total,), -1, jnp.int32).at[slot_position].set(crossing_segment)
    slotted_hyperedge = (
        jnp.full((slot_total,), -1, jnp.int32).at[slot_position].set(crossing_hyperedge)
    )
    members = (slotted_segment[None, :] == jnp.arange(seg, dtype=jnp.int32)[:, None]).astype(
        jnp.float32
    )
    degree = (MEM + jnp.sum(members, axis=1))[:, None]
    members = members.astype(jnp.bfloat16)

    def pick_slots(rows):
        return jnp.einsum("sn,sf->nf", members, rows, preferred_element_type=jnp.float32).astype(
            jnp.bfloat16
        )

    send = pick_slots(z)
    recv, recv_edge = (
        lax.all_to_all(send, ("region", "sub"), split_axis=0, concat_axis=0, tiled=True),
        lax.all_to_all(
            slotted_hyperedge, ("region", "sub"), split_axis=0, concat_axis=0, tiled=True
        ),
    )
    owned = (recv_edge[None, :] == edge_index[:, None]).astype(jnp.float32)
    count = 1.0 + inner_count + jnp.sum(owned, axis=1)
    owned = owned.astype(jnp.bfloat16)
    scale = (edge_weight / count)[:, None]

    def edge_side(local_rows, arrived):
        total = jnp.dot(incidence, local_rows, preferred_element_type=jnp.float32) + jnp.dot(
            owned, arrived, preferred_element_type=jnp.float32
        )
        values = (scale * total).astype(jnp.bfloat16)
        returned = jnp.einsum(
            "en,ef->nf", owned, values, preferred_element_type=jnp.float32
        ).astype(jnp.bfloat16)
        return (values, returned)

    def member_side(values, back):
        return jnp.einsum(
            "es,ef->sf", incidence, values, preferred_element_type=jnp.float32
        ) + jnp.dot(members, back, preferred_element_type=jnp.float32)

    edge_val, ret_rows = edge_side(z, recv)
    back = lax.all_to_all(ret_rows, ("region", "sub"), split_axis=0, concat_axis=0, tiled=True)
    y = member_side(edge_val, back) / degree
    sig_y = jax.nn.sigmoid(y)
    block_out = (y * sig_y).astype(jnp.bfloat16)
    dy = cotangent.astype(jnp.float32) * sig_y * (1.0 + y * (1.0 - sig_y))
    grad_rows = (dy / degree).astype(jnp.bfloat16)
    send_grads = pick_slots(grad_rows)
    recv_grads = lax.all_to_all(
        send_grads, ("region", "sub"), split_axis=0, concat_axis=0, tiled=True
    )
    dedge, ret_grads = edge_side(grad_rows, recv_grads)
    back_grads = lax.all_to_all(
        ret_grads, ("region", "sub"), split_axis=0, concat_axis=0, tiled=True
    )
    dz = member_side(dedge, back_grads).astype(jnp.bfloat16).reshape(seg, TP, B, C)
    g_theta = jnp.einsum("stbc,stbd->cd", hidden, dz, preferred_element_type=jnp.float32)
    dh = jnp.einsum("stbd,cd->stbc", dz, theta, preferred_element_type=jnp.float32)
    du = jnp.concatenate([dh * gate, dh * first * gate * (1.0 - gate)], axis=-1).astype(
        jnp.bfloat16
    )
    g_conv = jnp.einsum("stbk,stbf->kf", stack, du, preferred_element_type=jnp.float32)
    g_bias = jnp.sum(du.astype(jnp.float32), axis=(0, 1, 2))
    sum_conv, sum_bias, sum_theta = lax.psum((g_conv, g_bias, g_theta), ("region", "sub"))
    norm = 1.0 / jnp.sqrt(jnp.float32(seg * device_list * TP * B))
    dstack = jnp.einsum("stbf,kf->stbk", du, conv_weight, preferred_element_type=jnp.float32)
    grad_sum = jnp.zeros((seg, T_SIZE, B, C), jnp.float32)
    for k in range(KT):
        grad_sum = grad_sum + jnp.pad(
            dstack[..., k * C : (k + 1) * C], ((0, 0), (k, KT - 1 - k), (0, 0), (0, 0))
        )
    grad_feats = grad_sum.astype(jnp.bfloat16).reshape(seg, T_SIZE * B * C)
    return (block_out, grad_feats, sum_conv * norm, sum_bias * norm, sum_theta * norm)


def solution(mesh):
    in_specs = (
        P(("region", "sub"), None),
        P(),
        P(),
        P(),
        P(("region", "sub")),
        P(("region", "sub"), None),
        P(("region", "sub")),
        P(("region", "sub"), None),
        P(("region", "sub")),
        P(("region", "sub"), None),
    )
    out_specs = (P(("region", "sub"), None), P(("region", "sub"), None), P(), P(), P())
    return jax.shard_map(body, mesh=mesh, in_specs=in_specs, out_specs=out_specs, check_vma=False)
```

profile of v0, /device:TPU:8, one launch (start us, length us, event | category | flops | bytes accessed | tf_op | source)
XLA Modules:
  0.0 271.4 jit_solution(6056330176690974189)
XLA Ops:
  7.2 0.7 fusion.59
  8.1 0.8 select_reduce_fusion
  8.9 0.7 fusion.66
  9.6 1.1 scatter_custom_fusion
  10.7 0.7 all_to_all.38
  11.4 6.0 %all-to-all-start = ((s32[32,8,1]{1,2,0:T(1,128)}), s32[32,8,1]{1,2,0:T(1,128)S(1)}, u32[]{:S(2)}, u32[]{:S(2)}) async-start(s32[32,8,1]{1,2,0:T(1,128)} %bitcast.5), calls=%async_computation | async-start | bytes 32768 | tf_op jit(solution)/shard_map/all_to_all | solution.py:80
  17.5 1.1 scatter_custom_fusion.1
  18.6 1.7 copy.44
  20.3 0.5 fusion.72
  21.0 1.0 broadcast_add_fusion
  22.7 0.7 multiply_convert_fusion.3
  23.5 1.6 copy-done.1
  25.0 0.6 convolution_convert_fusion.4
  25.6 0.5 copy-done.2
  26.2 1.4 fusion.10
  27.6 5.8 %all-to-all-start.1 = ((bf16[32,8,1280]{2,1,0:T(8,128)(2,1)}), bf16[32,8,1280]{2,1,0:T(8,128)(2,1)S(1)}, u32[]{:S(2)}, u32[]{:S(2)}) async-start(bf16[32,8,1280]{2,1,0:T(8,128)(2,1)} %fusion.10), calls=%async_computation.1 | async-start | bytes 1310720 | tf_op jit(solution)/shard_map/all_to_all | solution.py:79
  33.6 0.6 fusion.45
  34.1 0.5 broadcast.65
  34.6 0.7 reduce.3
  35.6 15.4 %all-to-all-done.1 = bf16[32,8,1280]{2,1,0:T(8,128)(2,1)S(1)} async-done(((bf16[32,8,1280]{2,1,0:T(8,128)(2,1)}), bf16[32,8,1280]{2,1,0:T(8,128)(2,1)S(1)}, u32[]{:S(2)}, u32[]{:S(2)}) %all-to-all-start.1) | async-done | bytes 655392 | tf_op jit(solution)/shard_map/all_to_all | solution.py:79
  51.2 1.2 fusion.11
  52.4 3.8 %all-to-all-start.2 = ((bf16[32,8,1280]{2,1,0:T(8,128)(2,1)}), bf16[32,8,1280]{2,1,0:T(8,128)(2,1)S(1)}, u32[]{:S(2)}, u32[]{:S(2)}) async-start(bf16[32,8,1280]{2,1,0:T(8,128)(2,1)} %fusion.11), calls=%async_computation.2 | async-start | bytes 1310720 | tf_op jit(solution)/shard_map/all_to_all | solution.py:105
  56.5 2.0 fusion.43
  58.5 15.4 %all-to-all-done.2 = bf16[32,8,1280]{2,1,0:T(8,128)(2,1)S(1)} async-done(((bf16[32,8,1280]{2,1,0:T(8,128)(2,1)}), bf16[32,8,1280]{2,1,0:T(8,128)(2,1)S(1)}, u32[]{:S(2)}, u32[]{:S(2)}) %all-to-all-start.2) | async-done | bytes 655392 | tf_op jit(solution)/shard_map/all_to_all | solution.py:105
  73.9 4.1 %divide_convert_fusion = (bf16[512,1280]{1,0:T(8,128)(2,1)S(1)}, bf16[512,1280]{1,0:T(8,128)(2,1)}) fusion(bf16[512,1280]{1,0:T(8,128)(2,1)} %param.19, f32[512]{0:T(512)S(1)} %broadcast_add_fusion.1, f32[512,1280]{1,0:T(8,128)} %fusion.43, bf16[32,8,1280]{2,1,0:T(8,128)(2,1)S(1)} %all-to-all-done.2, s32[256]{0:T(256)S(1)} %scatter_custom_fusion.1), kind=kOutput, calls=%fused_computation.19 | convolution fusion | flops 345767936 | bytes 7212032 | tf_op jit(solution)/shard_map/dot_general | solution.py:102
  77.9 1.4 fusion.12
  79.3 3.8 %all-to-all-start.3 = ((bf16[32,8,1280]{2,1,0:T(8,128)(2,1)}), bf16[32,8,1280]{2,1,0:T(8,128)(2,1)S(1)}, u32[]{:S(2)}, u32[]{:S(2)}) async-start(bf16[32,8,1280]{2,1,0:T(8,128)(2,1)} %fusion.12), calls=%async_computation.3 | async-start | bytes 1310720 | tf_op jit(solution)/shard_map/all_to_all | solution.py:112
  83.5 17.2 %all-to-all-done.3 = bf16[32,8,1280]{2,1,0:T(8,128)(2,1)S(1)} async-done(((bf16[32,8,1280]{2,1,0:T(8,128)(2,1)}), bf16[32,8,1280]{2,1,0:T(8,128)(2,1)S(1)}, u32[]{:S(2)}, u32[]{:S(2)}) %all-to-all-start.3) | async-done | bytes 655392 | tf_op jit(solution)/shard_map/all_to_all | solution.py:112
  101.0 1.2 fusion.13
  102.2 3.9 %all-to-all-start.4 = ((bf16[32,8,1280]{2,1,0:T(8,128)(2,1)}), bf16[32,8,1280]{2,1,0:T(8,128)(2,1)}, u32[]{:S(2)}, u32[]{:S(2)}) async-start(bf16[32,8,1280]{2,1,0:T(8,128)(2,1)} %fusion.13), calls=%async_computation.4 | async-start | bytes 1310720 | tf_op jit(solution)/shard_map/all_to_all | solution.py:116
  106.3 0.5 fusion.39
  106.9 16.9 %all-to-all-done.4 = bf16[32,8,1280]{2,1,0:T(8,128)(2,1)} async-done(((bf16[32,8,1280]{2,1,0:T(8,128)(2,1)}), bf16[32,8,1280]{2,1,0:T(8,128)(2,1)}, u32[]{:S(2)}, u32[]{:S(2)}) %all-to-all-start.4) | async-done | bytes 655392 | tf_op jit(solution)/shard_map/all_to_all | solution.py:116
  123.8 2.7 fusion.3
  126.4 2.4 copy.46
  128.9 4.3 %multiply_convert_fusion.1 = (bf16[512,10,2,64]{0,3,2,1:T(8,128)(2,1)S(1)}, bf16[512,10,2,64]{0,3,2,1:T(8,128)(2,1)S(1)}) fusion(f32[512,10,2,128]{0,3,2,1:T(8,128)} %copy-done.1, bf16[512,10,2,64]{0,3,2,1:T(8,128)(2,1)} %bitcast.78, bf16[64,64]{1,0:T(8,128)(2,1)S(1)} %copy-done.11), kind=kOutput, calls=%fused_computation.18 | convolution fusion | flops 90439680 | bytes 9183232 | tf_op jit(solution)/shard_map/stbd,cd->stbc/dot_general | solution.py:121
  133.3 0.5 fusion.24
  133.8 0.8 copy-done.6
  134.9 1.8 fusion.19
  136.8 0.4 convert_reduce_fusion
  137.2 4.2 %fusion.60 = f32[512,10,2,192]{0,3,2,1:T(8,128)} fusion(bf16[192,128]{1,0:T(8,128)(2,1)S(1)} %copy-done, bf16[512,10,2,64]{0,3,2,1:T(8,128)(2,1)S(1)} %get-tuple-element.31, bf16[512,10,2,64]{0,3,2,1:T(8,128)(2,1)S(1)} %get-tuple-element.30), kind=kOutput, calls=%fused_computation.82 | convolution fusion | flops 508559360 | bytes 10534912 | tf_op jit(solution)/shard_map/stbf,kf->stbk/dot_general | solution.py:129
  141.5 39.5 %all-reduce.3 = (f32[128]{0:T(128)S(1)}, f32[64,64]{1,0:T(8,128)S(1)}) all-reduce(f32[128]{0:T(128)S(1)} %convert_reduce_fusion, f32[64,64]{1,0:T(8,128)S(1)} %fusion.24), channel_id=1, replica_groups=mesh['region'=4,'sub'=8] {'region','sub'}, use_global_device_ids=true, to_apply=%region_9.10 | all-reduce | flops 4224 | bytes 33792 | tf_op jit(solution)/shard_map/psum | solution.py:127
  181.0 0.5 broadcast_multiply_fusion.2
  181.5 0.6 broadcast_multiply_fusion.1
  182.2 4.4 %fusion.71 = (f32[512,10,2,64]{0,3,2,1:T(8,128)S(1)}, f32[512,10,2,64]{0,3,2,1:T(8,128)S(1)}, f32[512,10,2,64]{0,3,2,1:T(8,128)S(1)}) fusion(f32[512,10,2,192]{0,3,2,1:T(8,128)} %fusion.60), kind=kLoop, calls=%fused_computation.100 | loop fusion | bytes 15728640 | tf_op jit(solution)/shard_map/slice | solution.py:133
  186.6 1.0 add_convert_fusion
  187.6 1.6 copy.52
  189.2 73.8 %all-reduce.6.cloned.1.call-done = f32[192,128]{1,0:T(8,128)} async-done(((f32[192,128]{1,0:T(8,128)}), f32[192,128]{1,0:T(8,128)}) %all-reduce.6.cloned.1.call-update) | async-done | bytes 98320 | tf_op jit(solution)/shard_map/psum | solution.py:127
  263.0 1.5 broadcast_multiply_fusion
  (41 shorter events, 3.1 us)
Async XLA Ops:
  7.2 13.7 %copy-start = (bf16[192,128]{1,0:T(8,128)(2,1)S(1)}, bf16[192,128]{1,0:T(8,128)(2,1)}, u32[]{:S(2)}) copy-start(bf16[192,128]{1,0:T(8,128)(2,1)} %param.11) | copy-start | bytes 147460
  11.4 16.1 %all-to-all-start = ((s32[32,8,1]{1,2,0:T(1,128)}), s32[32,8,1]{1,2,0:T(1,128)S(1)}, u32[]{:S(2)}, u32[]{:S(2)}) async-start(s32[32,8,1]{1,2,0:T(1,128)} %bitcast.5), calls=%async_computation | async-start | bytes 32768 | tf_op jit(solution)/shard_map/all_to_all | solution.py:80
  20.3 0.7 copy-start.14
  20.8 1.2 copy-start.5
  20.8 1.5 copy-start.7
  20.8 1.9 copy-start.9
  22.7 2.3 copy-start.1
  22.7 2.3 copy-start.11
  25.0 1.1 copy-start.2
  25.0 8.4 %copy-start.12 = (s32[512,2]{0,1:T(2,128)S(1)}, s32[512,2]{0,1:T(2,128)}, u32[]{:S(2)}) copy-start(s32[512,2]{0,1:T(2,128)} %param.15) | copy-start | bytes 12292
  26.2 9.4 %copy-start.13 = (f32[128]{0:T(128)S(1)}, f32[128]{0:T(128)}, u32[]{:S(2)}) copy-start(f32[128]{0:T(128)} %param.14) | copy-start | bytes 1540
  27.6 23.4 %all-to-all-start.1 = ((bf16[32,8,1280]{2,1,0:T(8,128)(2,1)}), bf16[32,8,1280]{2,1,0:T(8,128)(2,1)S(1)}, u32[]{:S(2)}, u32[]{:S(2)}) async-start(bf16[32,8,1280]{2,1,0:T(8,128)(2,1)} %fusion.10), calls=%async_computation.1 | async-start | bytes 1310720 | tf_op jit(solution)/shard_map/all_to_all | solution.py:79
  52.4 21.4 %all-to-all-start.2 = ((bf16[32,8,1280]{2,1,0:T(8,128)(2,1)}), bf16[32,8,1280]{2,1,0:T(8,128)(2,1)S(1)}, u32[]{:S(2)}, u32[]{:S(2)}) async-start(bf16[32,8,1280]{2,1,0:T(8,128)(2,1)} %fusion.11), calls=%async_computation.2 | async-start | bytes 1310720 | tf_op jit(solution)/shard_map/all_to_all | solution.py:105
  79.3 21.4 %all-to-all-start.3 = ((bf16[32,8,1280]{2,1,0:T(8,128)(2,1)}), bf16[32,8,1280]{2,1,0:T(8,128)(2,1)S(1)}, u32[]{:S(2)}, u32[]{:S(2)}) async-start(bf16[32,8,1280]{2,1,0:T(8,128)(2,1)} %fusion.12), calls=%async_computation.3 | async-start | bytes 1310720 | tf_op jit(solution)/shard_map/all_to_all | solution.py:112
  102.2 21.5 %all-to-all-start.4 = ((bf16[32,8,1280]{2,1,0:T(8,128)(2,1)}), bf16[32,8,1280]{2,1,0:T(8,128)(2,1)}, u32[]{:S(2)}, u32[]{:S(2)}) async-start(bf16[32,8,1280]{2,1,0:T(8,128)(2,1)} %fusion.13), calls=%async_computation.4 | async-start | bytes 1310720 | tf_op jit(solution)/shard_map/all_to_all | solution.py:116
  106.1 156.9 %all-reduce.6.cloned.1.call-start = ((), (), s32[]{:S(2)}) async-start(), calls=%async_computation.5 | async-start | bytes 196608 | tf_op jit(solution)/shard_map/psum | solution.py:127
  128.9 4.4 %copy-start.3 = (bf16[512,10,2,64]{0,3,2,1:T(8,128)(2,1)S(1)}, bf16[512,10,2,64]{0,3,2,1:T(8,128)(2,1)}, u32[]{:S(2)}) copy-start(bf16[512,10,2,64]{0,3,2,1:T(8,128)(2,1)} %copy-done.2) | copy-start | bytes 3932164
  128.9 4.4 %copy-start.4 = (bf16[512,1280]{0,1:T(8,128)(2,1)S(1)}, bf16[512,1280]{0,1:T(8,128)(2,1)}, u32[]{:S(2)}) copy-start(bf16[512,1280]{0,1:T(8,128)(2,1)} %copy.46) | copy-start | bytes 3932164
  128.9 4.9 %copy-start.10 = (bf16[512,10,2,64]{0,3,2,1:T(8,128)(2,1)S(1)}, bf16[512,10,2,64]{0,3,2,1:T(8,128)(2,1)}, u32[]{:S(2)}) copy-start(bf16[512,10,2,64]{0,3,2,1:T(8,128)(2,1)} %copy-done.9) | copy-start | bytes 3932164
  133.2 1.3 copy-start.6
  133.2 1.7 copy-start.8
Sparse Core Ops, SparseCore 0:
  141.6 121.3 all-reduce.5
where the time goes:
time: 272 us; the launch traced here: 271 us
  waiting for transfers between devices  139 us (51%)
  blocking collectives  39.5 us (15%)
  matrix products  28.4 us (10%)
  starting transfers between devices  23.7 us (9%)
  local copies, waits for them, and re-layouts  18.3 us (7%)
  between operations  14.4 us (5%)
  other arithmetic  8.34 us (3%)
    psum x1, waiting for transfers between devices, body(): lax.psum((g_conv, g_bias, g_theta), ('region', 'sub'))  73.8 us
    psum x1, blocking collectives, body(): lax.psum((g_conv, g_bias, g_theta), ('region', 'sub'))  39.5 us
    all_to_all x1, waiting for transfers between devices, body(): lax.all_to_all(send_grads, ('region', 'sub'), split_axis=0, concat_axis=0...  17.2 us
    all_to_all x1, waiting for transfers between devices, body(): lax.all_to_all(ret_grads, ('region', 'sub'), split_axis=0, concat_axis=0,...  16.9 us
    all_to_all x1, waiting for transfers between devices, body(): lax.all_to_all(send, ('region', 'sub'), split_axis=0, concat_axis=0, tile...  15.4 us
    all_to_all x1, waiting for transfers between devices, body(): lax.all_to_all(ret_rows, ('region', 'sub'), split_axis=0, concat_axis=0,...  15.4 us
    unnamed x32, local copies, waits for them, and re-layouts  7.5 us
    dot_general x2, matrix products, member_side(): jnp.dot(members, back, preferred_element_type=jnp.float32)  6.71 us
  transfers between devices with their start and end apart: 6, of which 5 were waited for; matrix products, arithmetic and copies ran while one was open for 7% of the time, Pallas kernels for 0%

commit v1 on v0

--- a/solution.py
+++ b/solution.py
@@ -124,7 +124,7 @@
     )
     g_conv = jnp.einsum("stbk,stbf->kf", stack, du, preferred_element_type=jnp.float32)
     g_bias = jnp.sum(du.astype(jnp.float32), axis=(0, 1, 2))
-    sum_conv, sum_bias, sum_theta = lax.psum((g_conv, g_bias, g_theta), ("region", "sub"))
+    sum_conv, sum_bias, sum_theta = lax.psum(lax.psum((g_conv, g_bias, g_theta), "sub"), "region")
     norm = 1.0 / jnp.sqrt(jnp.float32(seg * device_list * TP * B))
     dstack = jnp.einsum("stbf,kf->stbk", du, conv_weight, preferred_element_type=jnp.float32)
     grad_sum = jnp.zeros((seg, T_SIZE, B, C), jnp.float32)

time: 272 us -> 240 us (0.88)
  waiting for transfers between devices: 139 us -> 98.6 us
  local copies, waits for them, and re-layouts: 18.3 us -> 22.1 us
  other arithmetic: 8.34 us -> 11.7 us
    psum x1 -> x2, waiting for transfers between devices: 73.8 us -> 33.7 us  [the longest x1 30.4 us: body(): lax.psum(lax.psum((g_conv, g_bias, g_theta), 'sub'), 'region')]
    convert_element_type x1, other arithmetic: 1 us -> 4.4 us  [body(): grad_feats = grad_sum.astype(jnp.bfloat16).reshape(seg, T_SIZE * B * C)]
    slice x1, local copies, waits for them, and re-layouts: 4.41 us -> 7.15 us  [body(): dstack[..., k * C:(k + 1) * C]]
    psum x1 -> x2, blocking collectives: 39.5 us -> 38.9 us  [the longest x1 22.7 us: body(): lax.psum((g_conv, g_bias, g_theta), 'sub')]
  transfers between devices with their start and end apart: 6 -> 7, of which waited for: 5 -> 6; matrix products, arithmetic and copies ran while one was open for 7% -> 12% of each run, Pallas kernels for 0% -> 0%
where the time goes in v1:
time: 240 us; the launch traced here: 238 us
  waiting for transfers between devices  98.6 us (41%)
  blocking collectives  38.9 us (16%)
  matrix products  28.4 us (12%)
  starting transfers between devices  23.7 us (10%)
  local copies, waits for them, and re-layouts  22.1 us (9%)
  between operations  14.4 us (6%)
  other arithmetic  11.7 us (5%)
    psum x1, waiting for transfers between devices, body(): lax.psum(lax.psum((g_conv, g_bias, g_theta), 'sub'), 'region')  30.4 us
    psum x1, blocking collectives, body(): lax.psum((g_conv, g_bias, g_theta), 'sub')  22.7 us
    all_to_all x1, waiting for transfers between devices, body(): lax.all_to_all(send_grads, ('region', 'sub'), split_axis=0, concat_axis=0...  17.2 us
    all_to_all x1, waiting for transfers between devices, body(): lax.all_to_all(ret_grads, ('region', 'sub'), split_axis=0, concat_axis=0,...  16.9 us
    psum x1, blocking collectives, body(): lax.psum(lax.psum((g_conv, g_bias, g_theta), 'sub'), 'region')  16.2 us
    all_to_all x1, waiting for transfers between devices, body(): lax.all_to_all(send, ('region', 'sub'), split_axis=0, concat_axis=0, tile...  15.4 us
    all_to_all x1, waiting for transfers between devices, body(): lax.all_to_all(ret_rows, ('region', 'sub'), split_axis=0, concat_axis=0,...  15.4 us
    unnamed x32, local copies, waits for them, and re-layouts  8.53 us
  transfers between devices with their start and end apart: 7, of which 6 were waited for; matrix products, arithmetic and copies ran while one was open for 12% of the time, Pallas kernels for 0%

profile of v1, /device:TPU:8, one launch (start us, length us, event | category | flops | bytes accessed | tf_op | source)
XLA Modules:
  0.0 237.8 jit_solution(9706555793400806454)
XLA Ops:
  7.2 0.7 fusion.59
  8.1 0.8 select_reduce_fusion
  8.9 0.7 fusion.66
  9.6 1.1 scatter_custom_fusion
  10.7 0.7 all_to_all.38
  11.4 6.0 %all-to-all-start = ((s32[32,8,1]{1,2,0:T(1,128)}), s32[32,8,1]{1,2,0:T(1,128)S(1)}, u32[]{:S(2)}, u32[]{:S(2)}) async-start(s32[32,8,1]{1,2,0:T(1,128)} %bitcast.5), calls=%async_computation | async-start | bytes 32768 | tf_op jit(solution)/shard_map/all_to_all | solution.py:80
  17.5 1.1 scatter_custom_fusion.1
  18.6 1.7 copy.44
  21.0 1.0 broadcast_add_fusion
  22.7 0.7 multiply_convert_fusion.3
  23.5 1.6 copy-done.1
  25.1 0.6 convolution_convert_fusion.4
  25.6 0.5 copy-done.2
  26.2 1.4 fusion.10
  27.6 5.8 %all-to-all-start.1 = ((bf16[32,8,1280]{2,1,0:T(8,128)(2,1)}), bf16[32,8,1280]{2,1,0:T(8,128)(2,1)S(1)}, u32[]{:S(2)}, u32[]{:S(2)}) async-start(bf16[32,8,1280]{2,1,0:T(8,128)(2,1)} %fusion.10), calls=%async_computation.1 | async-start | bytes 1310720 | tf_op jit(solution)/shard_map/all_to_all | solution.py:79
  33.6 0.6 fusion.45
  34.1 0.5 broadcast.65
  34.6 0.7 reduce.3
  35.6 15.4 %all-to-all-done.1 = bf16[32,8,1280]{2,1,0:T(8,128)(2,1)S(1)} async-done(((bf16[32,8,1280]{2,1,0:T(8,128)(2,1)}), bf16[32,8,1280]{2,1,0:T(8,128)(2,1)S(1)}, u32[]{:S(2)}, u32[]{:S(2)}) %all-to-all-start.1) | async-done | bytes 655392 | tf_op jit(solution)/shard_map/all_to_all | solution.py:79
  51.3 1.2 fusion.11
  52.5 3.8 %all-to-all-start.2 = ((bf16[32,8,1280]{2,1,0:T(8,128)(2,1)}), bf16[32,8,1280]{2,1,0:T(8,128)(2,1)S(1)}, u32[]{:S(2)}, u32[]{:S(2)}) async-start(bf16[32,8,1280]{2,1,0:T(8,128)(2,1)} %fusion.11), calls=%async_computation.2 | async-start | bytes 1310720 | tf_op jit(solution)/shard_map/all_to_all | solution.py:105
  56.5 2.1 fusion.43
  58.5 15.4 %all-to-all-done.2 = bf16[32,8,1280]{2,1,0:T(8,128)(2,1)S(1)} async-done(((bf16[32,8,1280]{2,1,0:T(8,128)(2,1)}), bf16[32,8,1280]{2,1,0:T(8,128)(2,1)S(1)}, u32[]{:S(2)}, u32[]{:S(2)}) %all-to-all-start.2) | async-done | bytes 655392 | tf_op jit(solution)/shard_map/all_to_all | solution.py:105
  73.9 4.0 %divide_convert_fusion = (bf16[512,1280]{1,0:T(8,128)(2,1)S(1)}, bf16[512,1280]{1,0:T(8,128)(2,1)}) fusion(bf16[512,1280]{1,0:T(8,128)(2,1)} %param.19, f32[512]{0:T(512)S(1)} %broadcast_add_fusion.1, f32[512,1280]{1,0:T(8,128)} %fusion.43, bf16[32,8,1280]{2,1,0:T(8,128)(2,1)S(1)} %all-to-all-done.2, s32[256]{0:T(256)S(1)} %scatter_custom_fusion.1), kind=kOutput, calls=%fused_computation.19 | convolution fusion | flops 345767936 | bytes 7212032 | tf_op jit(solution)/shard_map/dot_general | solution.py:102
  77.9 1.4 fusion.12
  79.3 3.8 %all-to-all-start.3 = ((bf16[32,8,1280]{2,1,0:T(8,128)(2,1)}), bf16[32,8,1280]{2,1,0:T(8,128)(2,1)S(1)}, u32[]{:S(2)}, u32[]{:S(2)}) async-start(bf16[32,8,1280]{2,1,0:T(8,128)(2,1)} %fusion.12), calls=%async_computation.3 | async-start | bytes 1310720 | tf_op jit(solution)/shard_map/all_to_all | solution.py:112
  83.5 17.2 %all-to-all-done.3 = bf16[32,8,1280]{2,1,0:T(8,128)(2,1)S(1)} async-done(((bf16[32,8,1280]{2,1,0:T(8,128)(2,1)}), bf16[32,8,1280]{2,1,0:T(8,128)(2,1)S(1)}, u32[]{:S(2)}, u32[]{:S(2)}) %all-to-all-start.3) | async-done | bytes 655392 | tf_op jit(solution)/shard_map/all_to_all | solution.py:112
  101.0 1.2 fusion.13
  102.2 3.9 %all-to-all-start.4 = ((bf16[32,8,1280]{2,1,0:T(8,128)(2,1)}), bf16[32,8,1280]{2,1,0:T(8,128)(2,1)}, u32[]{:S(2)}, u32[]{:S(2)}) async-start(bf16[32,8,1280]{2,1,0:T(8,128)(2,1)} %fusion.13), calls=%async_computation.4 | async-start | bytes 1310720 | tf_op jit(solution)/shard_map/all_to_all | solution.py:116
  106.4 0.5 fusion.39
  106.9 16.9 %all-to-all-done.4 = bf16[32,8,1280]{2,1,0:T(8,128)(2,1)} async-done(((bf16[32,8,1280]{2,1,0:T(8,128)(2,1)}), bf16[32,8,1280]{2,1,0:T(8,128)(2,1)}, u32[]{:S(2)}, u32[]{:S(2)}) %all-to-all-start.4) | async-done | bytes 655392 | tf_op jit(solution)/shard_map/all_to_all | solution.py:116
  123.8 2.7 %fusion.3 = bf16[512,1280]{1,0:T(8,128)(2,1)} fusion(f32[512,1280]{1,0:T(8,128)S(1)} %fusion.39, bf16[32,8,1280]{2,1,0:T(8,128)(2,1)} %all-to-all-done.4, s32[256]{0:T(256)S(1)} %scatter_custom_fusion.1), kind=kOutput, calls=%fused_computation.10 | convolution fusion | flops 337248256 | bytes 4588544 | tf_op jit(solution)/shard_map/dot_general | solution.py:102
  126.4 2.4 %copy.46 = bf16[512,1280]{0,1:T(8,128)(2,1)} copy(bf16[512,1280]{1,0:T(8,128)(2,1)} %fusion.3) | data formatting | bytes 2621440 | tf_op jit(solution)/shard_map/convert_element_type | solution.py:119
  128.9 4.4 %multiply_convert_fusion.1 = (bf16[512,10,2,64]{0,3,2,1:T(8,128)(2,1)S(1)}, bf16[512,10,2,64]{0,3,2,1:T(8,128)(2,1)S(1)}) fusion(f32[512,10,2,128]{0,3,2,1:T(8,128)} %copy-done.1, bf16[512,10,2,64]{0,3,2,1:T(8,128)(2,1)} %bitcast.78, bf16[64,64]{1,0:T(8,128)(2,1)S(1)} %copy-done.11), kind=kOutput, calls=%fused_computation.18 | convolution fusion | flops 90439680 | bytes 9183232 | tf_op jit(solution)/shard_map/stbd,cd->stbc/dot_general | solution.py:121
  133.3 0.5 fusion.24
  133.8 0.8 copy-done.6
  135.0 1.8 fusion.19
  137.2 4.3 %fusion.60 = f32[512,10,2,192]{0,3,2,1:T(8,128)} fusion(bf16[192,128]{1,0:T(8,128)(2,1)S(1)} %copy-done, bf16[512,10,2,64]{0,3,2,1:T(8,128)(2,1)S(1)} %get-tuple-element.33, bf16[512,10,2,64]{0,3,2,1:T(8,128)(2,1)S(1)} %get-tuple-element.32), kind=kOutput, calls=%fused_computation.82 | convolution fusion | flops 508559360 | bytes 10534912 | tf_op jit(solution)/shard_map/stbf,kf->stbk/dot_general | solution.py:129
  141.6 22.7 %all-reduce.3 = (f32[128]{0:T(128)S(1)}, f32[64,64]{1,0:T(8,128)S(1)}) all-reduce(f32[128]{0:T(128)S(1)} %convert_reduce_fusion, f32[64,64]{1,0:T(8,128)S(1)} %fusion.24), channel_id=1, replica_groups=mesh['region'=4,'sub'=8] {'sub'}, use_global_device_ids=true, to_apply=%region_10.11 | all-reduce | flops 4224 | bytes 33792 | tf_op jit(solution)/shard_map/psum | solution.py:127
  164.3 16.2 %all-reduce.4 = (f32[128]{0:T(128)S(1)}, f32[64,64]{1,0:T(8,128)S(1)}) all-reduce(f32[128]{0:T(128)S(1)} %get-tuple-element.25, f32[64,64]{1,0:T(8,128)S(1)} %get-tuple-element.26), channel_id=1, replica_groups=mesh['region'=4,'sub'=8] {'region'}, use_global_device_ids=true, to_apply=%region_11.12 | all-reduce | flops 4224 | bytes 33792 | tf_op jit(solution)/shard_map/psum | solution.py:127
  180.5 0.6 broadcast_multiply_fusion.1
  181.1 7.1 %fusion.71 = (f32[512,10,2,64]{0,3,2,1:T(8,128)S(1)}, f32[512,10,2,64]{0,3,2,1:T(8,128)}, f32[512,10,2,64]{0,3,2,1:T(8,128)}) fusion(f32[512,10,2,192]{0,3,2,1:T(8,128)} %fusion.60), kind=kLoop, calls=%fused_computation.100 | loop fusion | bytes 15728640 | tf_op jit(solution)/shard_map/slice | solution.py:133
  188.3 0.5 broadcast_multiply_fusion.2
  188.8 3.3 %all-reduce.8.cloned.1.call-done = f32[192,128]{1,0:T(8,128)} async-done(((f32[192,128]{1,0:T(8,128)}), f32[192,128]{1,0:T(8,128)}) %all-reduce.8.cloned.1.call-update) | async-done | bytes 98320 | tf_op jit(solution)/shard_map/psum | solution.py:127
  192.1 4.4 %add_convert_fusion = bf16[512,12,2,64]{0,3,2,1:T(8,128)(2,1)} fusion(f32[512,10,2,64]{0,3,2,1:T(8,128)} %get-tuple-element.30, f32[512,10,2,64]{0,3,2,1:T(8,128)} %get-tuple-element.31, f32[512,10,2,64]{0,3,2,1:T(8,128)S(1)} %get-tuple-element.29), kind=kLoop, calls=%fused_computation.9 | loop fusion | flops 2359296 | bytes 9437184 | tf_op jit(solution)/shard_map/convert_element_type | solution.py:135
  196.5 2.6 %copy.52 = bf16[512,1536]{1,0:T(8,128)(2,1)} copy(bf16[512,1536]{0,1:T(8,128)(2,1)} %bitcast.77) | data formatting | bytes 3145728
  199.1 30.4 %all-reduce.10.cloned.1.call-done = f32[192,128]{1,0:T(8,128)} async-done(((f32[192,128]{1,0:T(8,128)}), f32[192,128]{1,0:T(8,128)}) %all-reduce.10.cloned.1.call-update) | async-done | bytes 98320 | tf_op jit(solution)/shard_map/psum | solution.py:127
  229.5 1.5 broadcast_multiply_fusion
  (45 shorter events, 4.0 us)
Async XLA Ops:
  7.2 13.7 %copy-start = (bf16[192,128]{1,0:T(8,128)(2,1)S(1)}, bf16[192,128]{1,0:T(8,128)(2,1)}, u32[]{:S(2)}) copy-start(bf16[192,128]{1,0:T(8,128)(2,1)} %param.11) | copy-start | bytes 147460
  11.4 16.1 %all-to-all-start = ((s32[32,8,1]{1,2,0:T(1,128)}), s32[32,8,1]{1,2,0:T(1,128)S(1)}, u32[]{:S(2)}, u32[]{:S(2)}) async-start(s32[32,8,1]{1,2,0:T(1,128)} %bitcast.5), calls=%async_computation | async-start | bytes 32768 | tf_op jit(solution)/shard_map/all_to_all | solution.py:80
  20.3 0.7 copy-start.14
  20.8 1.2 copy-start.5
  20.8 1.6 copy-start.7
  20.8 1.9 copy-start.9
  22.7 2.3 copy-start.1
  22.7 2.3 copy-start.11
  25.0 1.1 copy-start.2
  25.1 8.4 %copy-start.12 = (s32[512,2]{0,1:T(2,128)S(1)}, s32[512,2]{0,1:T(2,128)}, u32[]{:S(2)}) copy-start(s32[512,2]{0,1:T(2,128)} %param.15) | copy-start | bytes 12292
  26.2 9.4 %copy-start.13 = (f32[128]{0:T(128)S(1)}, f32[128]{0:T(128)}, u32[]{:S(2)}) copy-start(f32[128]{0:T(128)} %param.14) | copy-start | bytes 1540
  27.6 23.4 %all-to-all-start.1 = ((bf16[32,8,1280]{2,1,0:T(8,128)(2,1)}), bf16[32,8,1280]{2,1,0:T(8,128)(2,1)S(1)}, u32[]{:S(2)}, u32[]{:S(2)}) async-start(bf16[32,8,1280]{2,1,0:T(8,128)(2,1)} %fusion.10), calls=%async_computation.1 | async-start | bytes 1310720 | tf_op jit(solution)/shard_map/all_to_all | solution.py:79
  52.5 21.4 %all-to-all-start.2 = ((bf16[32,8,1280]{2,1,0:T(8,128)(2,1)}), bf16[32,8,1280]{2,1,0:T(8,128)(2,1)S(1)}, u32[]{:S(2)}, u32[]{:S(2)}) async-start(bf16[32,8,1280]{2,1,0:T(8,128)(2,1)} %fusion.11), calls=%async_computation.2 | async-start | bytes 1310720 | tf_op jit(solution)/shard_map/all_to_all | solution.py:105
  79.3 21.4 %all-to-all-start.3 = ((bf16[32,8,1280]{2,1,0:T(8,128)(2,1)}), bf16[32,8,1280]{2,1,0:T(8,128)(2,1)S(1)}, u32[]{:S(2)}, u32[]{:S(2)}) async-start(bf16[32,8,1280]{2,1,0:T(8,128)(2,1)} %fusion.12), calls=%async_computation.3 | async-start | bytes 1310720 | tf_op jit(solution)/shard_map/all_to_all | solution.py:112
  102.2 21.5 %all-to-all-start.4 = ((bf16[32,8,1280]{2,1,0:T(8,128)(2,1)}), bf16[32,8,1280]{2,1,0:T(8,128)(2,1)}, u32[]{:S(2)}, u32[]{:S(2)}) async-start(bf16[32,8,1280]{2,1,0:T(8,128)(2,1)} %fusion.13), calls=%async_computation.4 | async-start | bytes 1310720 | tf_op jit(solution)/shard_map/all_to_all | solution.py:116
  106.1 85.9 %all-reduce.8.cloned.1.call-start = ((), (), s32[]{:S(2)}) async-start(), calls=%async_computation.5 | async-start | bytes 196608 | tf_op jit(solution)/shard_map/psum | solution.py:127
  128.9 4.4 %copy-start.3 = (bf16[512,10,2,64]{0,3,2,1:T(8,128)(2,1)S(1)}, bf16[512,10,2,64]{0,3,2,1:T(8,128)(2,1)}, u32[]{:S(2)}) copy-start(bf16[512,10,2,64]{0,3,2,1:T(8,128)(2,1)} %copy-done.2) | copy-start | bytes 3932164
  128.9 4.4 %copy-start.4 = (bf16[512,1280]{0,1:T(8,128)(2,1)S(1)}, bf16[512,1280]{0,1:T(8,128)(2,1)}, u32[]{:S(2)}) copy-start(bf16[512,1280]{0,1:T(8,128)(2,1)} %copy.46) | copy-start | bytes 3932164
  128.9 4.9 %copy-start.10 = (bf16[512,10,2,64]{0,3,2,1:T(8,128)(2,1)S(1)}, bf16[512,10,2,64]{0,3,2,1:T(8,128)(2,1)}, u32[]{:S(2)}) copy-start(bf16[512,10,2,64]{0,3,2,1:T(8,128)(2,1)} %copy-done.9) | copy-start | bytes 3932164
  133.3 1.3 copy-start.6
  133.3 1.7 copy-start.8
  141.5 88.0 %all-reduce.10.cloned.1.call-start = ((), (), s32[]{:S(2)}) async-start(), calls=%async_computation.6 | async-start | bytes 196608 | tf_op jit(solution)/shard_map/psum | solution.py:127
Sparse Core Ops, SparseCore 0:
  141.6 50.3 all-reduce.7
  194.5 34.9 all-reduce.9
